TPU v7x, 32 devices: a whole 2x2x4 slice. The times are simulated.
32 devices in a mesh: ep: 16 (over z, x, core), dp: 2 (over y).
Axes of the slice: x: 2, y: 2, z: 4, core: 2. Of those that a mesh axis runs over, the one named last changes fastest.
Arguments:
- tokens: bfloat16 [1024, 4096], P('ep', 'dp'), may hold values from -6 to 6
- expert_ids: int32 [1024, 8], P('ep'), may hold values from 0 to 15, all different within a row
- gate_logits: float32 [1024, 8], P('ep'), may hold values from -6 to 6
- placement: int32 [8], replicated, may hold values from 0 to 15, as said below
- split_rows: int32 [8], replicated, may hold values from 0 to 32
- gate_up_weight: bfloat16 [16, 4096, 2, 1024], P('ep', None, None, 'dp'), may hold values from -0.09375 to 0.09375
- down_weight: bfloat16 [16, 1024, 4096], P('ep', None, 'dp'), may hold values from -0.1875 to 0.1875
- spare_gate_up: bfloat16 [16, 4096, 2, 512], P('ep', None, None, 'dp'), may hold values from -0.09375 to 0.09375
- spare_down: bfloat16 [16, 512, 4096], P('ep', None, 'dp'), may hold values from -0.1875 to 0.1875
Outputs:
- mixed: bfloat16 [1024, 4096], P('ep', 'dp')
Inputs may be any that keep to these rules, and one draw needn't show every extreme that they name: `expert_ids`: each token names 8 different experts. `placement`: 8 different experts.
All inputs are finite; a program needn't handle non-finite values.
Results may differ from a plain program's by a relative error of at most 0.0058.
Values may be sent and summed in bfloat16 or wider, within the bound.
No kernel may reach another device: no remote copies, remote signals or barrier semaphores. Data moves between devices by JAX's collectives and lax.ppermute only.
A program may use at most 64 MiB of HBM per device.

v0:
```python
import jax
import jax.numpy as jnp
from jax import lax
from jax.sharding import PartitionSpec as P


def gate_up(row_block, weight):
    gate_both = jnp.einsum("rd,djf->rjf", row_block, weight, preferred_element_type=jnp.float32)
    return (jax.nn.silu(gate_both[:, 0, :]) * gate_both[:, 1, :]).astype(jnp.bfloat16)


def slot_tables(ids, target, low, limit, capacity, top_count):
    groups, per_group = ids.shape
    hit = ids == target
    ordinal = jnp.arange(per_group, dtype=jnp.int32)
    earlier = (ordinal[None, :] < ordinal[:, None]).astype(jnp.bfloat16)
    rank = jnp.einsum(
        "pq,gq->gp", earlier, hit.astype(jnp.bfloat16), preferred_element_type=jnp.float32
    ).astype(jnp.int32)
    position = rank - low
    kept = hit & (position >= 0) & (position < limit)
    group_tokens = per_group // top_count
    token = (
        jnp.arange(groups, dtype=jnp.int32)[:, None] * group_tokens + ordinal[None, :] // top_count
    )
    slots = jnp.arange(capacity, dtype=jnp.int32)
    sel = kept[:, :, None] & (position[:, :, None] == slots[None, None, :])
    row_of_slot = jnp.sum(jnp.where(sel, token[:, :, None], 0), axis=1)
    flat = jnp.arange(groups, dtype=jnp.int32)[:, None] * capacity + position
    return (row_of_slot.reshape(-1), kept, flat)


def per_token(kept, flat, weight, group_tokens, top_count):
    groups = kept.shape[0]
    kept = kept.reshape(groups * group_tokens, top_count)
    flat = flat.reshape(groups * group_tokens, top_count)
    index = jnp.sum(jnp.where(kept, flat, 0), axis=1)
    scale = jnp.sum(jnp.where(kept, weight, 0.0), axis=1)
    return (index, scale)


def per_device(
    tokens,
    expert_ids,
    gate_logits,
    placement,
    split_rows,
    gate_up_weight,
    down_weight,
    spare_gate_up,
    spare_down,
):
    ep_count = lax.axis_size("ep")
    me = lax.axis_index("ep")
    group_tokens = tokens.shape[0]
    top_count = expert_ids.shape[1]
    spares = placement.shape[0]
    halves = spare_gate_up.shape[0] * ep_count // spares
    capacity = group_tokens * top_count // ep_count
    per_group = group_tokens * top_count
    whole_rows = lax.all_gather(tokens, "dp", axis=1, tiled=True)
    every_row = lax.all_gather(whole_rows, "ep", axis=0, tiled=True)
    every_id = lax.all_gather(expert_ids, "ep", axis=0, tiled=True)
    every_logit = lax.all_gather(gate_logits, "ep", axis=0, tiled=True)
    ids = every_id.reshape(ep_count, per_group)
    gate_score = jax.nn.sigmoid(every_logit)
    gate_weight = 2.5 * gate_score / jnp.sum(gate_score, axis=1, keepdims=True)
    is_match = placement == me
    home_limit = jnp.where(
        jnp.any(is_match),
        jnp.minimum(jnp.sum(jnp.where(is_match, split_rows, 0)), capacity),
        capacity,
    )
    home_rows_of, home_kept, home_flat = slot_tables(ids, me, 0, home_limit, capacity, top_count)
    spare_index = me // halves
    spare_rows_of, spare_kept, spare_flat = slot_tables(
        ids, placement[spare_index], split_rows[spare_index], capacity, capacity, top_count
    )
    home_rows = jnp.take(every_row, home_rows_of, axis=0)
    spare_rows = jnp.take(every_row, spare_rows_of, axis=0)
    home_hidden = gate_up(home_rows, gate_up_weight[0])
    spare_hidden = gate_up(spare_rows, spare_gate_up[0])
    home_hidden = lax.all_gather(home_hidden, "dp", axis=1, tiled=True)
    spare_hidden = lax.all_gather(spare_hidden, "dp", axis=1, tiled=True)
    home_out = jnp.dot(home_hidden, down_weight[0], preferred_element_type=jnp.float32)
    home_out = home_out.astype(jnp.bfloat16).astype(jnp.float32)
    spare_out = jnp.dot(spare_hidden, spare_down[0], preferred_element_type=jnp.float32)
    home_at, home_scale = per_token(home_kept, home_flat, gate_weight, group_tokens, top_count)
    spare_at, spare_scale = per_token(spare_kept, spare_flat, gate_weight, group_tokens, top_count)
    partial = home_scale[:, None] * jnp.take(home_out, home_at, axis=0) + spare_scale[
        :, None
    ] * jnp.take(spare_out, spare_at, axis=0)
    mixed = lax.psum_scatter(partial, "ep", scatter_dimension=0, tiled=True)
    return mixed.astype(jnp.bfloat16)


def solution(mesh):
    return jax.shard_map(
        per_device,
        mesh=mesh,
        in_specs=(
            P("ep", "dp"),
            P("ep", None),
            P("ep", None),
            P(),
            P(),
            P("ep", None, None, "dp"),
            P("ep", None, "dp"),
            P("ep", None, None, "dp"),
            P("ep", None, "dp"),
        ),
        out_specs=P("ep", "dp"),
        check_vma=False,
    )
```

profile of v0, /device:TPU:0, one launch (start us, length us, event | category | flops | bytes accessed | tf_op | source)
XLA Modules:
  0.0 299.5 jit_solution(7959396471671987635)
XLA Ops:
  6.5 12.0 %all_gather.20 = bf16[64,4096]{1,0:T(8,128)(2,1)} all-gather(bf16[64,2048]{1,0:T(8,128)(2,1)} %param.13), channel_id=1, replica_groups=mesh['ep'=16,'dp'=2] {'dp'}, dimensions={1}, use_global_device_ids=true | all-gather | bytes 786432 | tf_op jit(solution)/shard_map/all_gather | solution.py:61
  18.6 1.2 dynamic_slice.6
  19.9 1.3 dynamic_slice.7
  21.2 22.4 %all-gather = s32[16,64,8]{1,2,0:T(8,128)S(1)} all-gather(s32[1,64,8]{1,2,0:T(8,128)} %bitcast.64), channel_id=1, replica_groups=mesh['ep'=16,'dp'=2] {'ep'}, dimensions={0}, use_global_device_ids=true | all-gather | bytes 34816 | tf_op jit(solution)/shard_map/all_gather | solution.py:63
  44.8 0.9 compare_and_fusion
  46.1 1.3 fusion.37
  48.1 1.3 compare_reduce_fusion
  51.6 18.5 %all-gather.1 = f32[16,64,8]{1,2,0:T(8,128)S(1)} all-gather(f32[1,64,8]{1,2,0:T(8,128)} %bitcast.65), channel_id=1, replica_groups=mesh['ep'=16,'dp'=2] {'ep'}, dimensions={0}, use_global_device_ids=true | all-gather | bytes 34816 | tf_op jit(solution)/shard_map/all_gather | solution.py:64
  70.2 1.1 copy.33
  72.5 1.5 select_reduce_fusion.5
  74.1 20.5 %all-gather.5.cloned.1.call-done = bf16[1024,4096]{1,0:T(8,128)(2,1)} async-done(((bf16[64,4096]{1,0:T(8,128)(2,1)}), bf16[1024,4096]{1,0:T(8,128)(2,1)}) %all-gather.5.cloned.1.call-update) | async-done | bytes 8388624 | tf_op jit(solution)/shard_map/all_gather | solution.py:62
  94.6 13.0 %gather_fusion = bf16[512,4096]{1,0:T(8,128)(2,1)} fusion(bf16[1024,4096]{1,0:T(8,128)(2,1)} %all-gather.5.cloned.1.call-done, s32[1024]{0:T(1024)S(1)} %pad_clamp_fusion.1), kind=kCustom, calls=%fused_computation.clone | custom fusion | bytes 8390656 | tf_op jit(solution)/shard_map/jit(_take)/gather | solution.py:79
  107.7 8.3 %fusion = f32[512,2,512]{2,0,1:T(8,128)S(1)} fusion(bf16[4096,2,512]{2,1,0:T(2,128)(2,1)} %bitcast.66, bf16[512,4096]{1,0:T(8,128)(2,1)} %gather_fusion, pred[512]{0:T(512)(128)(4,1)S(1)} %compare_and_fusion.5), kind=kOutput, calls=%fused_computation.4 | convolution fusion | flops 4297064448 | bytes 14680576 | tf_op jit(solution)/shard_map/rd,djf->rjf/dot_general | solution.py:8
  116.0 1.1 fusion.25
  117.3 13.0 %gather_fusion.2 = bf16[512,4096]{1,0:T(8,128)(2,1)} fusion(bf16[1024,4096]{1,0:T(8,128)(2,1)} %all-gather.5.cloned.1.call-done, s32[1024]{0:T(1024)S(1)} %pad_clamp_fusion), kind=kCustom, calls=%fused_computation.2.clone | custom fusion | bytes 8390656 | tf_op jit(solution)/shard_map/jit(_take)/gather | solution.py:80
  130.4 5.8 %fusion.3 = f32[512,2,256]{2,0,1:T(8,128)S(1)} fusion(bf16[4096,2,256]{2,1,0:T(2,128)(2,1)} %bitcast.67, bf16[512,4096]{1,0:T(8,128)(2,1)} %gather_fusion.2, pred[512]{0:T(512)(128)(4,1)S(1)} %compare_and_fusion.4), kind=kOutput, calls=%fused_computation.9 | convolution fusion | flops 2149580800 | bytes 9437696 | tf_op jit(solution)/shard_map/rd,djf->rjf/dot_general | solution.py:8
  136.4 9.4 %all_gather.23 = bf16[512,512]{1,0:T(8,128)(2,1)S(1)} all-gather(bf16[512,256]{1,0:T(8,128)(2,1)S(1)} %fusion.29), channel_id=1, replica_groups=mesh['ep'=16,'dp'=2] {'dp'}, dimensions={1}, use_global_device_ids=true | all-gather | bytes 786432 | tf_op jit(solution)/shard_map/all_gather | solution.py:84
  145.7 3.3 %fusion.19 = f32[512,2048]{1,0:T(8,128)} fusion(bf16[512,512]{1,0:T(8,128)(2,1)S(1)} %all_gather.23, bf16[1,512,2048]{2,1,0:T(8,128)(2,1)S(1)} %copy-done), kind=kOutput, calls=%fused_computation.21 | convolution fusion | flops 1073741824 | bytes 6815744 | tf_op jit(solution)/shard_map/dot_general | solution.py:87
  149.0 11.2 %gather_fusion.3 = f32[1024,2048]{1,0:T(8,128)} fusion(f32[512,2048]{1,0:T(8,128)} %fusion.19, s32[1024]{0:T(1024)S(1)} %fusion.33), kind=kCustom, calls=%fused_computation.3.clone | custom fusion | bytes 16781312 | tf_op jit(solution)/shard_map/jit(_take)/gather | solution.py:92
  160.2 6.8 %fusion.16 = f32[512,2048]{1,0:T(8,128)} fusion(bf16[512,1024]{1,0:T(8,128)(2,1)} %all-gather.7.cloned.1.call-done, bf16[1,1024,2048]{2,1,0:T(8,128)(2,1)} %param.19), kind=kOutput, calls=%fused_computation.20 | convolution fusion | flops 2149580800 | bytes 9437184 | tf_op jit(solution)/shard_map/dot_general | solution.py:85
  167.0 11.3 %gather_fusion.1 = f32[1024,2048]{1,0:T(8,128)} fusion(f32[512,2048]{1,0:T(8,128)} %fusion.16, s32[1024]{0:T(1024)S(1)} %fusion.32), kind=kCustom, calls=%fused_computation.1.clone | custom fusion | bytes 16781312 | tf_op jit(solution)/shard_map/jit(_take)/gather | solution.py:90
  178.2 9.9 %fusion.2 = f32[1024,2048]{1,0:T(8,128)} fusion(f32[1024,2048]{1,0:T(8,128)} %gather_fusion.3, f32[1024,2048]{1,0:T(8,128)} %gather_fusion.1, f32[1024]{0:T(1024)S(1)} %get-tuple-element.8, f32[1024]{0:T(1024)S(1)} %get-tuple-element.6, pred[1024]{0:T(1024)(128)(4,1)S(1)} %get-tuple-element.19, pred[1024]{0:T(1024)(128)(4,1)S(1)} %get-tuple-element.20), kind=kLoop, calls=%fused_computation.7 | loop fusion | flops 10485760 | bytes 25176064 | tf_op jit(solution)/shard_map/add | solution.py:90
  188.2 103.1 %reduce-scatter.2.cloned.1.call-done = f32[64,2048]{1,0:T(8,128)} async-done(((f32[1024,2048]{1,0:T(8,128)}), f32[64,2048]{1,0:T(8,128)}) %reduce-scatter.2.cloned.1.call-update) | async-done | bytes 524304 | tf_op jit(solution)/shard_map/reduce_scatter | solution.py:93
  291.2 1.8 convert_element_type.31
  (45 shorter events, 5.0 us)
Async XLA Ops:
  6.5 139.2 %copy-start = (bf16[1,512,2048]{2,1,0:T(8,128)(2,1)S(1)}, bf16[1,512,2048]{2,1,0:T(8,128)(2,1)}, u32[]{:S(2)}) copy-start(bf16[1,512,2048]{2,1,0:T(8,128)(2,1)} %param.21) | copy-start | bytes 6291460
  6.5 88.1 %all-gather.5.cloned.1.call-start = ((), (), s32[]{:S(2)}) async-start(), calls=%async_computation.1 | async-start | bytes 8912896 | tf_op jit(solution)/shard_map/all_gather | solution.py:62
  18.6 141.6 %all-gather.7.cloned.1.call-start = ((), (), s32[]{:S(2)}) async-start(), calls=%async_computation.2 | async-start | bytes 1572864 | tf_op jit(solution)/shard_map/all_gather | solution.py:83
  117.1 174.1 %reduce-scatter.2.cloned.1.call-start = ((), (), s32[]{:S(2)}) async-start(), calls=%async_computation.3 | async-start | bytes 8912896 | tf_op jit(solution)/shard_map/reduce_scatter | solution.py:93
  188.1 104.9 %copy-start.1 = (bf16[1,512,2048]{2,1,0:T(8,128)(2,1)S(1)}, bf16[1,512,2048]{2,1,0:T(8,128)(2,1)}, u32[]{:S(2)}) copy-start(bf16[1,512,2048]{2,1,0:T(8,128)(2,1)} %param.21) | copy-start | bytes 6291460
Sparse Core Ops, SparseCore 0:
  18.7 75.8 all-gather.4
  117.2 19.5 all-gather.6
  188.3 102.8 reduce-scatter.1
where the time goes:
time: 300 us
  waiting for transfers between devices  124 us (41%)
  blocking collectives  62.2 us (21%)
  local copies, waits for them, and re-layouts  54.2 us (18%)
  matrix products  25.4 us (8%)
  other arithmetic  19.1 us (6%)
  between operations  14.6 us (5%)
    reduce_scatter x1, waiting for transfers between devices, per_device(): mixed = lax.psum_scatter(partial, 'ep', scatter_dimension=0, tiled=True)  103 us
    all_gather x1, blocking collectives, per_device(): every_id = lax.all_gather(expert_ids, 'ep', axis=0, tiled=True)  22.4 us
    all_gather x1, waiting for transfers between devices, per_device(): every_row = lax.all_gather(whole_rows, 'ep', axis=0, tiled=True)  20.5 us
    all_gather x1, blocking collectives, per_device(): every_logit = lax.all_gather(gate_logits, 'ep', axis=0, tiled=True)  18.5 us
    dot_general x2, matrix products, gate_up(): jnp.einsum('rd,djf->rjf', row_block, weight, preferred_element_type=jnp.f...  14.2 us
    gather x1, local copies, waits for them, and re-layouts, per_device(): spare_rows = jnp.take(every_row, spare_rows_of, axis=0)  13 us
    gather x1, local copies, waits for them, and re-layouts, per_device(): home_rows = jnp.take(every_row, home_rows_of, axis=0)  13 us
    all_gather x1, blocking collectives, per_device(): whole_rows = lax.all_gather(tokens, 'dp', axis=1, tiled=True)  12 us
  transfers between devices with their start and end apart: 3, of which 2 were waited for; matrix products, arithmetic and copies ran while one was open for 16% of the time, Pallas kernels for 0%

commit v1 on v0

--- a/solution.py
+++ b/solution.py
@@ -59,7 +59,12 @@
     capacity = group_tokens * top_count // ep_count
     per_group = group_tokens * top_count
     whole_rows = lax.all_gather(tokens, "dp", axis=1, tiled=True)
-    every_row = lax.all_gather(whole_rows, "ep", axis=0, tiled=True)
+    ring = [whole_rows]
+    for hop in range(15):
+        ring.append(lax.ppermute(ring[-1], "ep", [(dev, (dev + 1) % 16) for dev in range(16)]))
+    every_row = jnp.roll(
+        jnp.concatenate(ring[::-1], axis=0), (lax.axis_index("ep") + 1) * ring[0].shape[0], axis=0
+    )
     every_id = lax.all_gather(expert_ids, "ep", axis=0, tiled=True)
     every_logit = lax.all_gather(gate_logits, "ep", axis=0, tiled=True)
     ids = every_id.reshape(ep_count, per_group)

time: 300 us -> 470 us (1.57)
  waiting for transfers between devices: 124 us -> 240 us
  local copies, waits for them, and re-layouts: 54.2 us -> 111 us
  blocking collectives: 62.2 us -> 55.8 us
    ppermute x0 -> x15, waiting for transfers between devices: none -> 138 us  [per_device(): lax.ppermute(ring[-1], 'ep', [(dev, (dev + 1) % 16) for dev in range(16)])]
    unnamed x4 -> x67, local copies, waits for them, and re-layouts: 0.01 us -> 47.5 us
    all_gather x1 -> x0, waiting for transfers between devices: 20.5 us -> none  [per_device(): every_row = lax.all_gather(whole_rows, 'ep', axis=0, tiled=True)]
    dynamic_slice x0 -> x1, local copies, waits for them, and re-layouts: none -> 7.73 us  [per_device(): jnp.roll(jnp.concatenate(ring[::-1], axis=0), (lax.axis_index('ep') + 1)...]
  transfers between devices with their start and end apart: 3 -> 17, of which waited for: 2 -> 14; matrix products, arithmetic and copies ran while one was open for 16% -> 10% of each run, Pallas kernels for 0% -> 0%
where the time goes in v1:
time: 470 us; the launch traced here: 469 us
  waiting for transfers between devices  240 us (51%)
  local copies, waits for them, and re-layouts  111 us (24%)
  blocking collectives  55.8 us (12%)
  matrix products  25.4 us (5%)
  other arithmetic  20.5 us (4%)
  between operations  15 us (3%)
    ppermute x15, waiting for transfers between devices, per_device(): lax.ppermute(ring[-1], 'ep', [(dev, (dev + 1) % 16) for dev in range(16)])  138 us
    reduce_scatter x1, waiting for transfers between devices, per_device(): mixed = lax.psum_scatter(partial, 'ep', scatter_dimension=0, tiled=True)  102 us
    unnamed x67, local copies, waits for them, and re-layouts  47.5 us
    all_gather x1, blocking collectives, per_device(): every_id = lax.all_gather(expert_ids, 'ep', axis=0, tiled=True)  19.7 us
    all_gather x1, blocking collectives, per_device(): every_logit = lax.all_gather(gate_logits, 'ep', axis=0, tiled=True)  18.4 us
    dot_general x2, matrix products, gate_up(): jnp.einsum('rd,djf->rjf', row_block, weight, preferred_element_type=jnp.f...  14.2 us
    gather x1, local copies, waits for them, and re-layouts, per_device(): spare_rows = jnp.take(every_row, spare_rows_of, axis=0)  13.1 us
    gather x1, local copies, waits for them, and re-layouts, per_device(): home_rows = jnp.take(every_row, home_rows_of, axis=0)  13 us
  transfers between devices with their start and end apart: 17, of which 14 were waited for; matrix products, arithmetic and copies ran while one was open for 10% of the time, Pallas kernels for 0%

profile of v1, /device:TPU:0, one launch (start us, length us, event | category | flops | bytes accessed | tf_op | source)
XLA Modules:
  0.0 468.8 jit_solution(8179244283210899003)
XLA Ops:
  6.5 10.3 %all_gather.17 = bf16[64,4096]{1,0:T(8,128)(2,1)S(1)} all-gather(bf16[64,2048]{1,0:T(8,128)(2,1)} %param.13), channel_id=1, replica_groups=mesh['ep'=16,'dp'=2] {'dp'}, dimensions={1}, use_global_device_ids=true | all-gather | bytes 786432 | tf_op jit(solution)/shard_map/all_gather | solution.py:61
  16.9 11.3 %collective-permute-done = bf16[64,4096]{1,0:T(8,128)(2,1)S(1)} collective-permute-done((bf16[64,4096]{1,0:T(8,128)(2,1)S(1)}, bf16[64,4096]{1,0:T(8,128)(2,1)S(1)}, u32[]{:S(2)}, u32[]{:S(2)}) %collective-permute-start) | collective-permute-done | bytes 524320 | tf_op jit(solution)/shard_map/ppermute | solution.py:64
  29.0 11.3 %collective-permute-done.1 = bf16[64,4096]{1,0:T(8,128)(2,1)S(1)} collective-permute-done((bf16[64,4096]{1,0:T(8,128)(2,1)S(1)}, bf16[64,4096]{1,0:T(8,128)(2,1)S(1)}, u32[]{:S(2)}, u32[]{:S(2)}) %collective-permute-start.1) | collective-permute-done | bytes 524320 | tf_op jit(solution)/shard_map/ppermute | solution.py:64
  41.1 11.3 %collective-permute-done.2 = bf16[64,4096]{1,0:T(8,128)(2,1)S(1)} collective-permute-done((bf16[64,4096]{1,0:T(8,128)(2,1)S(1)}, bf16[64,4096]{1,0:T(8,128)(2,1)S(1)}, u32[]{:S(2)}, u32[]{:S(2)}) %collective-permute-start.2) | collective-permute-done | bytes 524320 | tf_op jit(solution)/shard_map/ppermute | solution.py:64
  53.2 11.3 %collective-permute-done.3 = bf16[64,4096]{1,0:T(8,128)(2,1)S(1)} collective-permute-done((bf16[64,4096]{1,0:T(8,128)(2,1)S(1)}, bf16[64,4096]{1,0:T(8,128)(2,1)S(1)}, u32[]{:S(2)}, u32[]{:S(2)}) %collective-permute-start.3) | collective-permute-done | bytes 524320 | tf_op jit(solution)/shard_map/ppermute | solution.py:64
  65.3 11.3 %collective-permute-done.4 = bf16[64,4096]{1,0:T(8,128)(2,1)S(1)} collective-permute-done((bf16[64,4096]{1,0:T(8,128)(2,1)S(1)}, bf16[64,4096]{1,0:T(8,128)(2,1)S(1)}, u32[]{:S(2)}, u32[]{:S(2)}) %collective-permute-start.4) | collective-permute-done | bytes 524320 | tf_op jit(solution)/shard_map/ppermute | solution.py:64
  77.5 11.3 %collective-permute-done.5 = bf16[64,4096]{1,0:T(8,128)(2,1)S(1)} collective-permute-done((bf16[64,4096]{1,0:T(8,128)(2,1)S(1)}, bf16[64,4096]{1,0:T(8,128)(2,1)S(1)}, u32[]{:S(2)}, u32[]{:S(2)}) %collective-permute-start.5) | collective-permute-done | bytes 524320 | tf_op jit(solution)/shard_map/ppermute | solution.py:64
  89.6 11.3 %collective-permute-done.6 = bf16[64,4096]{1,0:T(8,128)(2,1)S(1)} collective-permute-done((bf16[64,4096]{1,0:T(8,128)(2,1)S(1)}, bf16[64,4096]{1,0:T(8,128)(2,1)S(1)}, u32[]{:S(2)}, u32[]{:S(2)}) %collective-permute-start.6) | collective-permute-done | bytes 524320 | tf_op jit(solution)/shard_map/ppermute | solution.py:64
  102.2 19.7 %all-gather = s32[16,64,8]{1,2,0:T(8,128)S(1)} all-gather(s32[1,64,8]{1,2,0:T(8,128)} %bitcast.64), channel_id=1, replica_groups=mesh['ep'=16,'dp'=2] {'ep'}, dimensions={0}, use_global_device_ids=true | all-gather | bytes 34816 | tf_op jit(solution)/shard_map/all_gather | solution.py:68
  134.5 10.5 %collective-permute-done.9 = bf16[64,4096]{1,0:T(8,128)(2,1)S(1)} collective-permute-done((bf16[64,4096]{1,0:T(8,128)(2,1)}, bf16[64,4096]{1,0:T(8,128)(2,1)S(1)}, u32[]{:S(2)}, u32[]{:S(2)}) %collective-permute-start.9) | collective-permute-done | bytes 524320 | tf_op jit(solution)/shard_map/ppermute | solution.py:64
  146.2 11.0 %collective-permute-done.10 = bf16[64,4096]{1,0:T(8,128)(2,1)} collective-permute-done((bf16[64,4096]{1,0:T(8,128)(2,1)S(1)}, bf16[64,4096]{1,0:T(8,128)(2,1)}, u32[]{:S(2)}, u32[]{:S(2)}) %collective-permute-start.10) | collective-permute-done | bytes 524320 | tf_op jit(solution)/shard_map/ppermute | solution.py:64
  160.2 18.4 %all-gather.1 = f32[16,64,8]{1,2,0:T(8,128)S(1)} all-gather(f32[1,64,8]{1,2,0:T(8,128)} %bitcast.65), channel_id=1, replica_groups=mesh['ep'=16,'dp'=2] {'ep'}, dimensions={0}, use_global_device_ids=true | all-gather | bytes 34816 | tf_op jit(solution)/shard_map/all_gather | solution.py:69
  183.1 10.1 %collective-permute-done.12 = bf16[64,4096]{1,0:T(8,128)(2,1)S(1)} collective-permute-done((bf16[64,4096]{1,0:T(8,128)(2,1)}, bf16[64,4096]{1,0:T(8,128)(2,1)S(1)}, u32[]{:S(2)}, u32[]{:S(2)}) %collective-permute-start.12) | collective-permute-done | bytes 524320 | tf_op jit(solution)/shard_map/ppermute | solution.py:64
  193.4 11.0 %collective-permute-done.13 = bf16[64,4096]{1,0:T(8,128)(2,1)S(1)} collective-permute-done((bf16[64,4096]{1,0:T(8,128)(2,1)S(1)}, bf16[64,4096]{1,0:T(8,128)(2,1)S(1)}, u32[]{:S(2)}, u32[]{:S(2)}) %collective-permute-start.13) | collective-permute-done | bytes 524320 | tf_op jit(solution)/shard_map/ppermute | solution.py:64
  204.5 11.3 %collective-permute-done.14 = bf16[64,4096]{1,0:T(8,128)(2,1)S(1)} collective-permute-done((bf16[64,4096]{1,0:T(8,128)(2,1)S(1)}, bf16[64,4096]{1,0:T(8,128)(2,1)S(1)}, u32[]{:S(2)}, u32[]{:S(2)}) %collective-permute-start.14) | collective-permute-done | bytes 524320 | tf_op jit(solution)/shard_map/ppermute | solution.py:64
  258.5 7.7 %constant_dynamic-slice_fusion = bf16[1024,4096]{1,0:T(8,128)(2,1)} fusion(bf16[2048,4096]{1,0:T(8,128)(2,1)} %constant_dynamic-update-slice_fusion, s32[]{:T(128)S(6)} %select_n.81), kind=kLoop, calls=%fused_computation.114 | loop fusion | bytes 16777220 | tf_op jit(solution)/shard_map/jit(_roll_dynamic)/dynamic_slice | solution.py:65
  266.2 13.0 %gather_fusion = bf16[512,4096]{1,0:T(8,128)(2,1)} fusion(bf16[1024,4096]{1,0:T(8,128)(2,1)} %constant_dynamic-slice_fusion, s32[1024]{0:T(1024)S(1)} %get-tuple-element.20), kind=kCustom, calls=%fused_computation.clone | custom fusion | bytes 8390656 | tf_op jit(solution)/shard_map/jit(_take)/gather | solution.py:84
  279.2 8.3 %fusion = f32[512,2,512]{2,0,1:T(8,128)S(1)} fusion(bf16[4096,2,512]{2,1,0:T(2,128)(2,1)} %bitcast.66, bf16[512,4096]{1,0:T(8,128)(2,1)} %gather_fusion, pred[512]{0:T(512)(128)(4,1)S(1)} %compare_and_fusion.5), kind=kOutput, calls=%fused_computation.4 | convolution fusion | flops 4297064448 | bytes 14680576 | tf_op jit(solution)/shard_map/rd,djf->rjf/dot_general | solution.py:8
  289.0 13.1 %gather_fusion.2 = bf16[512,4096]{1,0:T(8,128)(2,1)} fusion(bf16[1024,4096]{1,0:T(8,128)(2,1)} %constant_dynamic-slice_fusion, s32[1024]{0:T(1024)S(1)} %get-tuple-element.19), kind=kCustom, calls=%fused_computation.2.clone | custom fusion | bytes 8390656 | tf_op jit(solution)/shard_map/jit(_take)/gather | solution.py:85
  308.1 7.3 %all_gather.19 = bf16[512,512]{1,0:T(8,128)(2,1)S(1)} all-gather(bf16[512,256]{1,0:T(8,128)(2,1)S(1)} %fusion.29), channel_id=1, replica_groups=mesh['ep'=16,'dp'=2] {'dp'}, dimensions={1}, use_global_device_ids=true | all-gather | bytes 786432 | tf_op jit(solution)/shard_map/all_gather | solution.py:89
  318.7 11.2 %gather_fusion.3 = f32[1024,2048]{1,0:T(8,128)} fusion(f32[512,2048]{1,0:T(8,128)} %fusion.19, s32[1024]{0:T(1024)S(1)} %get-tuple-element.22), kind=kCustom, calls=%fused_computation.3.clone | custom fusion | bytes 16781312 | tf_op jit(solution)/shard_map/jit(_take)/gather | solution.py:97
  336.7 11.2 %gather_fusion.1 = f32[1024,2048]{1,0:T(8,128)} fusion(f32[512,2048]{1,0:T(8,128)} %fusion.16, s32[1024]{0:T(1024)S(1)} %get-tuple-element.21), kind=kCustom, calls=%fused_computation.1.clone | custom fusion | bytes 16781312 | tf_op jit(solution)/shard_map/jit(_take)/gather | solution.py:95
  347.9 10.1 %fusion.2 = f32[1024,2048]{1,0:T(8,128)} fusion(f32[1024,2048]{1,0:T(8,128)} %gather_fusion.3, f32[1024,2048]{1,0:T(8,128)} %gather_fusion.1, f32[1024]{0:T(1024)S(1)} %get-tuple-element.8, f32[1024]{0:T(1024)S(1)} %get-tuple-element.6, pred[1024]{0:T(1024)(128)(4,1)S(1)} %get-tuple-element.23, pred[1024]{0:T(1024)(128)(4,1)S(1)} %get-tuple-element.24), kind=kLoop, calls=%fused_computation.7 | loop fusion | flops 10485760 | bytes 25176064 | tf_op jit(solution)/shard_map/add | solution.py:95
  358.0 102.2 %reduce-scatter.2.cloned.1.call-done = f32[64,2048]{1,0:T(8,128)} async-done(((f32[1024,2048]{1,0:T(8,128)}), f32[64,2048]{1,0:T(8,128)}) %reduce-scatter.2.cloned.1.call-update) | async-done | bytes 524304 | tf_op jit(solution)/shard_map/reduce_scatter | solution.py:98
  (135 shorter events, 88.1 us)
Async XLA Ops:
  6.5 308.9 %copy-start = (bf16[1,512,2048]{2,1,0:T(8,128)(2,1)S(1)}, bf16[1,512,2048]{2,1,0:T(8,128)(2,1)}, u32[]{:S(2)}) copy-start(bf16[1,512,2048]{2,1,0:T(8,128)(2,1)} %param.21) | copy-start | bytes 6291460
  6.5 323.4 %all-gather.4.cloned.1.call-start = ((), (), s32[]{:S(2)}) async-start(), calls=%async_computation.1 | async-start | bytes 1572864 | tf_op jit(solution)/shard_map/all_gather | solution.py:88
  16.9 11.3 %collective-permute-start = (bf16[64,4096]{1,0:T(8,128)(2,1)S(1)}, bf16[64,4096]{1,0:T(8,128)(2,1)S(1)}, u32[]{:S(2)}, u32[]{:S(2)}) collective-permute-start(bf16[64,4096]{1,0:T(8,128)(2,1)S(1)} %all_gather.17), channel_id=1, source_target_pairs={{0,2},{2,4},{4,6},{6,8},{8,10},{10,12},{12,14},{14,16},{16,18},{18... | collective-permute-start | bytes 1572872 | tf_op jit(solution)/shard_map/ppermute | solution.py:64
  29.0 11.3 %collective-permute-start.1 = (bf16[64,4096]{1,0:T(8,128)(2,1)S(1)}, bf16[64,4096]{1,0:T(8,128)(2,1)S(1)}, u32[]{:S(2)}, u32[]{:S(2)}) collective-permute-start(bf16[64,4096]{1,0:T(8,128)(2,1)S(1)} %collective-permute-done), channel_id=1, source_target_pairs={{0,2},{2,4},{4,6},{6,8},{8,10},{10,12},{12,14},{14,16},{16,18},{18... | collective-permute-start | bytes 1572872 | tf_op jit(solution)/shard_map/ppermute | solution.py:64
  41.1 11.3 %collective-permute-start.2 = (bf16[64,4096]{1,0:T(8,128)(2,1)S(1)}, bf16[64,4096]{1,0:T(8,128)(2,1)S(1)}, u32[]{:S(2)}, u32[]{:S(2)}) collective-permute-start(bf16[64,4096]{1,0:T(8,128)(2,1)S(1)} %collective-permute-done.1), channel_id=1, source_target_pairs={{0,2},{2,4},{4,6},{6,8},{8,10},{10,12},{12,14},{14,16},{16,18},{18... | collective-permute-start | bytes 1572872 | tf_op jit(solution)/shard_map/ppermute | solution.py:64
  53.2 11.3 %collective-permute-start.3 = (bf16[64,4096]{1,0:T(8,128)(2,1)S(1)}, bf16[64,4096]{1,0:T(8,128)(2,1)S(1)}, u32[]{:S(2)}, u32[]{:S(2)}) collective-permute-start(bf16[64,4096]{1,0:T(8,128)(2,1)S(1)} %collective-permute-done.2), channel_id=1, source_target_pairs={{0,2},{2,4},{4,6},{6,8},{8,10},{10,12},{12,14},{14,16},{16,18},{18... | collective-permute-start | bytes 1572872 | tf_op jit(solution)/shard_map/ppermute | solution.py:64
  65.3 11.3 %collective-permute-start.4 = (bf16[64,4096]{1,0:T(8,128)(2,1)S(1)}, bf16[64,4096]{1,0:T(8,128)(2,1)S(1)}, u32[]{:S(2)}, u32[]{:S(2)}) collective-permute-start(bf16[64,4096]{1,0:T(8,128)(2,1)S(1)} %collective-permute-done.3), channel_id=1, source_target_pairs={{0,2},{2,4},{4,6},{6,8},{8,10},{10,12},{12,14},{14,16},{16,18},{18... | collective-permute-start | bytes 1572872 | tf_op jit(solution)/shard_map/ppermute | solution.py:64
  77.5 11.3 %collective-permute-start.5 = (bf16[64,4096]{1,0:T(8,128)(2,1)S(1)}, bf16[64,4096]{1,0:T(8,128)(2,1)S(1)}, u32[]{:S(2)}, u32[]{:S(2)}) collective-permute-start(bf16[64,4096]{1,0:T(8,128)(2,1)S(1)} %collective-permute-done.4), channel_id=1, source_target_pairs={{0,2},{2,4},{4,6},{6,8},{8,10},{10,12},{12,14},{14,16},{16,18},{18... | collective-permute-start | bytes 1572872 | tf_op jit(solution)/shard_map/ppermute | solution.py:64
  89.6 11.3 %collective-permute-start.6 = (bf16[64,4096]{1,0:T(8,128)(2,1)S(1)}, bf16[64,4096]{1,0:T(8,128)(2,1)S(1)}, u32[]{:S(2)}, u32[]{:S(2)}) collective-permute-start(bf16[64,4096]{1,0:T(8,128)(2,1)S(1)} %collective-permute-done.5), channel_id=1, source_target_pairs={{0,2},{2,4},{4,6},{6,8},{8,10},{10,12},{12,14},{14,16},{16,18},{18... | collective-permute-start | bytes 1572872 | tf_op jit(solution)/shard_map/ppermute | solution.py:64
  100.9 21.0 %collective-permute-start.7 = (bf16[64,4096]{1,0:T(8,128)(2,1)S(1)}, bf16[64,4096]{1,0:T(8,128)(2,1)}, u32[]{:S(2)}, u32[]{:S(2)}) collective-permute-start(bf16[64,4096]{1,0:T(8,128)(2,1)S(1)} %collective-permute-done.6), channel_id=1, source_target_pairs={{0,2},{2,4},{4,6},{6,8},{8,10},{10,12},{12,14},{14,16},{16,18},{18... | collective-permute-start | bytes 1572872 | tf_op jit(solution)/shard_map/ppermute | solution.py:64
  121.9 11.6 %collective-permute-start.8 = (bf16[64,4096]{1,0:T(8,128)(2,1)}, bf16[64,4096]{1,0:T(8,128)(2,1)}, u32[]{:S(2)}, u32[]{:S(2)}) collective-permute-start(bf16[64,4096]{1,0:T(8,128)(2,1)} %collective-permute-done.7), channel_id=1, source_target_pairs={{0,2},{2,4},{4,6},{6,8},{8,10},{10,12},{12,14},{14,16},{16,18},{18... | collective-permute-start | bytes 1572872 | tf_op jit(solution)/shard_map/ppermute | solution.py:64
  133.5 11.5 %collective-permute-start.9 = (bf16[64,4096]{1,0:T(8,128)(2,1)}, bf16[64,4096]{1,0:T(8,128)(2,1)S(1)}, u32[]{:S(2)}, u32[]{:S(2)}) collective-permute-start(bf16[64,4096]{1,0:T(8,128)(2,1)} %collective-permute-done.8), channel_id=1, source_target_pairs={{0,2},{2,4},{4,6},{6,8},{8,10},{10,12},{12,14},{14,16},{16,18},{18... | collective-permute-start | bytes 1572872 | tf_op jit(solution)/shard_map/ppermute | solution.py:64
  145.8 11.4 %collective-permute-start.10 = (bf16[64,4096]{1,0:T(8,128)(2,1)S(1)}, bf16[64,4096]{1,0:T(8,128)(2,1)}, u32[]{:S(2)}, u32[]{:S(2)}) collective-permute-start(bf16[64,4096]{1,0:T(8,128)(2,1)S(1)} %collective-permute-done.9), channel_id=1, source_target_pairs={{0,2},{2,4},{4,6},{6,8},{8,10},{10,12},{12,14},{14,16},{16,18},{18... | collective-permute-start | bytes 1572872 | tf_op jit(solution)/shard_map/ppermute | solution.py:64
  157.3 24.3 %collective-permute-start.11 = (bf16[64,4096]{1,0:T(8,128)(2,1)}, bf16[64,4096]{1,0:T(8,128)(2,1)}, u32[]{:S(2)}, u32[]{:S(2)}) collective-permute-start(bf16[64,4096]{1,0:T(8,128)(2,1)} %collective-permute-done.10), channel_id=1, source_target_pairs={{0,2},{2,4},{4,6},{6,8},{8,10},{10,12},{12,14},{14,16},{16,18},{18... | collective-permute-start | bytes 1572872 | tf_op jit(solution)/shard_map/ppermute | solution.py:64
  179.9 72.6 %copy-start.13 = (bf16[64,4096]{1,0:T(8,128)(2,1)S(1)}, bf16[64,4096]{1,0:T(8,128)(2,1)}, u32[]{:S(2)}) copy-start(bf16[64,4096]{1,0:T(8,128)(2,1)} %copy-done.12) | copy-start | bytes 1572868
  179.9 73.5 %copy-start.11 = (bf16[64,4096]{1,0:T(8,128)(2,1)S(1)}, bf16[64,4096]{1,0:T(8,128)(2,1)}, u32[]{:S(2)}) copy-start(bf16[64,4096]{1,0:T(8,128)(2,1)} %copy-done.10) | copy-start | bytes 1572868
  179.9 74.3 %copy-start.9 = (bf16[64,4096]{1,0:T(8,128)(2,1)S(1)}, bf16[64,4096]{1,0:T(8,128)(2,1)}, u32[]{:S(2)}) copy-start(bf16[64,4096]{1,0:T(8,128)(2,1)} %copy-done.8) | copy-start | bytes 1572868
  179.9 75.2 %copy-start.7 = (bf16[64,4096]{1,0:T(8,128)(2,1)S(1)}, bf16[64,4096]{1,0:T(8,128)(2,1)}, u32[]{:S(2)}) copy-start(bf16[64,4096]{1,0:T(8,128)(2,1)} %copy-done.6) | copy-start | bytes 1572868
  179.9 76.0 %copy-start.5 = (bf16[64,4096]{1,0:T(8,128)(2,1)S(1)}, bf16[64,4096]{1,0:T(8,128)(2,1)}, u32[]{:S(2)}) copy-start(bf16[64,4096]{1,0:T(8,128)(2,1)} %copy-done.4) | copy-start | bytes 1572868
  181.6 11.6 %collective-permute-start.12 = (bf16[64,4096]{1,0:T(8,128)(2,1)}, bf16[64,4096]{1,0:T(8,128)(2,1)S(1)}, u32[]{:S(2)}, u32[]{:S(2)}) collective-permute-start(bf16[64,4096]{1,0:T(8,128)(2,1)} %collective-permute-done.11), channel_id=1, source_target_pairs={{0,2},{2,4},{4,6},{6,8},{8,10},{10,12},{12,14},{14,16},{16,18},{18... | collective-permute-start | bytes 1572872 | tf_op jit(solution)/shard_map/ppermute | solution.py:64
  193.2 11.3 %collective-permute-start.13 = (bf16[64,4096]{1,0:T(8,128)(2,1)S(1)}, bf16[64,4096]{1,0:T(8,128)(2,1)S(1)}, u32[]{:S(2)}, u32[]{:S(2)}) collective-permute-start(bf16[64,4096]{1,0:T(8,128)(2,1)S(1)} %collective-permute-done.12), channel_id=1, source_target_pairs={{0,2},{2,4},{4,6},{6,8},{8,10},{10,12},{12,14},{14,16},{16,18},{18... | collective-permute-start | bytes 1572872 | tf_op jit(solution)/shard_map/ppermute | solution.py:64
  204.5 11.3 %collective-permute-start.14 = (bf16[64,4096]{1,0:T(8,128)(2,1)S(1)}, bf16[64,4096]{1,0:T(8,128)(2,1)S(1)}, u32[]{:S(2)}, u32[]{:S(2)}) collective-permute-start(bf16[64,4096]{1,0:T(8,128)(2,1)S(1)} %collective-permute-done.13), channel_id=1, source_target_pairs={{0,2},{2,4},{4,6},{6,8},{8,10},{10,12},{12,14},{14,16},{16,18},{18... | collective-permute-start | bytes 1572872 | tf_op jit(solution)/shard_map/ppermute | solution.py:64
  288.7 171.4 %reduce-scatter.2.cloned.1.call-start = ((), (), s32[]{:S(2)}) async-start(), calls=%async_computation.2 | async-start | bytes 8912896 | tf_op jit(solution)/shard_map/reduce_scatter | solution.py:98
  347.9 114.1 %copy-start.1 = (bf16[1,512,2048]{2,1,0:T(8,128)(2,1)S(1)}, bf16[1,512,2048]{2,1,0:T(8,128)(2,1)}, u32[]{:S(2)}) copy-start(bf16[1,512,2048]{2,1,0:T(8,128)(2,1)} %param.21) | copy-start | bytes 6291460
  (11 other events, 262.9 us)
Sparse Core Ops, SparseCore 0:
  288.9 21.1 all-gather.3
  358.1 102.0 reduce-scatter.1
